TPU v7x, 512 devices: a whole 4x8x8 slice. The times are simulated.
512 devices in a mesh: dp: 4 (over y_lo, core), seq: 4 (over x), fsdp: 32 (over y_hi, z).
Axes of the slice: x: 4, y: 8 (y_hi: 4, y_lo: 2; y = y_hi * 2 + y_lo), z: 8, core: 2. Of those that a mesh axis runs over, the one named last changes fastest.
Arguments:
- patches: bfloat16 [128, 768, 6144], P(('dp', 'fsdp'), 'seq'), may hold values from -100 to 100
- segments: int32 [128, 768], P(('dp', 'fsdp'), 'seq'), may hold values from 0 to 7, never falling along the last dimension, each value on 1 to 384 neighbouring positions
- qkv_weight: bfloat16 [6144, 384], P('fsdp'), may hold values from -0.078125 to 0.078125
- cotangent: bfloat16 [128, 768, 128], P(('dp', 'fsdp'), 'seq'), may hold values from -6 to 6
Outputs:
- input_grad: bfloat16 [128, 768, 6144], P(('dp', 'fsdp'), 'seq')
- weight_grad: float32 [6144, 384], P('fsdp')
Inputs may be any that keep to these rules, and one draw needn't show every extreme that they name: `segments`: within a sequence the image number never falls; each of the 8 images has 1 to 384 patches and one has exactly 384.
All inputs are finite; a program needn't handle non-finite values.
Results may differ from a plain program's by a relative error of at most 0.034.
The roundings to bfloat16 on the way count: a program that leaves them out, or rounds other values in their place, can miss the bound.
Values may be sent and summed in bfloat16 or wider, within the bound.
No kernel may reach another device: no remote copies, remote signals or barrier semaphores. Data moves between devices by JAX's collectives and lax.ppermute only.
A program may use at most 64 MiB of HBM per device.

v0:
```python
import jax
import jax.numpy as jnp
from jax import lax
from jax.sharding import PartitionSpec as P


def contract_first(left, right):
    return lax.dot_general(
        left, right, (((0,), (0,)), ((), ())), preferred_element_type=jnp.float32
    )


def contract_last(left, right):
    return lax.dot_general(
        left, right, (((1,), (1,)), ((), ())), preferred_element_type=jnp.float32
    )


def shards(patches, segments, qkv_weight, cotangent):
    features = patches[0]
    image_ids = segments[0]
    grad_out = cotangent[0]
    width_head = cotangent.shape[2]
    scale = width_head ** (-0.5)
    full_weight = lax.all_gather(qkv_weight, "fsdp", axis=0, tiled=True)
    projected = jnp.dot(features, full_weight, preferred_element_type=jnp.float32)
    heads = projected.astype(jnp.bfloat16)
    query = heads[:, :width_head]
    own_pairs = heads[:, width_head:]
    pairs_all, images_all = (
        lax.all_gather(own_pairs, "seq", axis=0, tiled=True),
        lax.all_gather(image_ids, "seq", axis=0, tiled=True),
    )
    keys_all = pairs_all[:, :width_head]
    values_all = pairs_all[:, width_head:]
    scores = contract_last(query, keys_all) * scale
    allowed = image_ids[:, None] == images_all[None, :]
    highest = jnp.max(jnp.where(allowed, scores, -jnp.inf), axis=1)
    summed = jnp.sum(jnp.where(allowed, jnp.exp(scores - highest[:, None]), 0.0), axis=1)
    log_total = highest + jnp.log(summed)
    attention = jnp.where(allowed, jnp.exp(scores - log_total[:, None]), 0.0)
    attention_low = attention.astype(jnp.bfloat16)
    output = jnp.dot(attention_low, values_all, preferred_element_type=jnp.float32)
    delta_rows = jnp.sum(grad_out.astype(jnp.float32) * output, axis=1)
    grad_attention = contract_last(grad_out, values_all)
    grad_scores = (attention * (grad_attention - delta_rows[:, None]) * scale).astype(jnp.bfloat16)
    grad_query = jnp.dot(grad_scores, keys_all, preferred_element_type=jnp.float32).astype(
        jnp.bfloat16
    )
    partial_pairs = jnp.concatenate(
        [contract_first(grad_scores, query), contract_first(attention_low, grad_out)], axis=1
    )
    grad_pairs = lax.psum_scatter(
        partial_pairs.astype(jnp.bfloat16), "seq", scatter_dimension=0, tiled=True
    )
    grad_heads = jnp.concatenate([grad_query, grad_pairs], axis=1)
    columns = lax.all_to_all(features, "fsdp", split_axis=1, concat_axis=0, tiled=True)
    partial_grad = contract_first(columns, lax.all_gather(grad_heads, "fsdp", axis=0, tiled=True))
    input_grad = contract_last(grad_heads, full_weight).astype(jnp.bfloat16)
    weight_grad = lax.psum(partial_grad.astype(jnp.bfloat16), ("dp", "seq")).astype(jnp.float32)
    return (input_grad[None], weight_grad)


def solution(mesh):
    placed = (
        P(("dp", "fsdp"), "seq", None),
        P(("dp", "fsdp"), "seq"),
        P("fsdp", None),
        P(("dp", "fsdp"), "seq", None),
    )
    return jax.shard_map(
        shards,
        mesh=mesh,
        in_specs=placed,
        out_specs=(P(("dp", "fsdp"), "seq", None), P("fsdp", None)),
        check_vma=False,
    )
```

profile of v0, /device:TPU:1, one launch (start us, length us, event | category | flops | bytes accessed | tf_op | source)
XLA Modules:
  0.0 472.2 jit_solution(8760330779892001765)
XLA Ops:
  7.2 0.7 all-gather.4.cloned.1.call-update
  7.9 1.3 dynamic-slice
  9.9 0.9 dynamic-update-slice
  10.8 7.7 %all-reduce = s32[768]{0:T(1024)S(1)} all-reduce(s32[768]{0:T(1024)S(1)} %dynamic-update-slice), channel_id=2, replica_groups=mesh['dp'=4,'seq'=4,'fsdp'=32] {'seq'}, use_global_device_ids=true, to_apply=%add | all-reduce | flops 768 | bytes 6144
  18.5 103.9 %all-gather.4.cloned.1.call-done = bf16[6144,384]{1,0:T(8,128)(2,1)} async-done(((bf16[192,384]{1,0:T(8,128)(2,1)}), bf16[6144,384]{1,0:T(8,128)(2,1)}) %all-gather.4.cloned.1.call-update) | async-done | bytes 4718608 | tf_op jit(solution)/shard_map/all_gather | solution.py:25
  122.4 4.4 fusion.7
  126.8 9.9 %all_gather.14 = bf16[768,256]{1,0:T(8,128)(2,1)S(1)} all-gather(bf16[192,256]{1,0:T(8,128)(2,1)S(1)} %slice.17), channel_id=1, replica_groups=mesh['dp'=4,'seq'=4,'fsdp'=32] {'seq'}, dimensions={0}, use_global_device_ids=true | all-gather | bytes 491520 | tf_op jit(solution)/shard_map/all_gather | solution.py:31
  136.8 0.3 fusion.12
  137.1 0.3 fusion.13
  137.9 0.3 fusion.11
  138.2 0.3 fusion.6
  138.8 0.9 copy.13
  140.1 23.7 %reduce-scatter.4.cloned.1.call-done = bf16[192,256]{1,0:T(8,128)(2,1)} async-done(((bf16[768,256]{1,0:T(8,128)(2,1)}), bf16[192,256]{1,0:T(8,128)(2,1)}) %reduce-scatter.4.cloned.1.call-update) | async-done | bytes 98320
  163.9 1.0 copy.14
  164.9 0.8 copy.10
  165.8 3.0 copy.11
  168.8 104.7 %all_to_all.19 = bf16[192,32,192]{0,2,1:T(8,128)(2,1)S(1)} all-to-all(bf16[192,32,192]{0,2,1:T(8,128)(2,1)S(1)} %bitcast.39), channel_id=1, replica_groups=mesh['dp'=4,'seq'=4,'fsdp'=32] {'fsdp'}, dimensions={1} | all-to-all | bytes 4718592 | tf_op jit(solution)/shard_map/all_to_all | solution.py:57
  273.5 1.8 copy.12
  275.2 4.2 all_to_all.17
  279.5 57.0 %all-gather.6.cloned.1.call-done = bf16[6144,384]{1,0:T(8,128)(2,1)} async-done(((bf16[192,384]{1,0:T(8,128)(2,1)}), bf16[6144,384]{1,0:T(8,128)(2,1)}) %all-gather.6.cloned.1.call-update) | async-done | bytes 4718608 | tf_op jit(solution)/shard_map/all_gather | solution.py:58
  336.4 5.1 %fusion.10 = bf16[192,384]{1,0:T(8,128)(2,1)} fusion(bf16[6144,192]{0,1:T(8,128)(2,1)} %all_to_all.17, bf16[6144,384]{1,0:T(8,128)(2,1)} %all-gather.6.cloned.1.call-done), kind=kOutput, calls=%fused_computation.14 | convolution fusion | flops 906043392 | bytes 7225344 | tf_op jit(solution)/shard_map/dot_general | solution.py:8
  341.5 5.6 %fusion = bf16[1,192,6144]{2,1,0:T(8,128)(2,1)} fusion(bf16[6144,384]{1,0:T(8,128)(2,1)} %all-gather.4.cloned.1.call-done, bf16[192,256]{0,1:T(8,128)(2,1)S(1)} %copy.14, bf16[192,128]{0,1:T(8,128)(2,1)S(1)} %copy.9), kind=kOutput, calls=%fused_computation.1 | convolution fusion | flops 907444224 | bytes 7225344 | tf_op jit(solution)/shard_map/dot_general | solution.py:14
  347.2 116.8 %all-reduce.3.cloned.1.call-done = bf16[192,384]{1,0:T(8,128)(2,1)} async-done(((bf16[192,384]{1,0:T(8,128)(2,1)}), bf16[192,384]{1,0:T(8,128)(2,1)}) %all-reduce.3.cloned.1.call-update) | async-done | bytes 147472 | tf_op jit(solution)/shard_map/psum | solution.py:60
  464.0 1.6 convert_element_type.36
  (21 shorter events, 1.3 us)
Async XLA Ops:
  7.2 115.2 %all-gather.4.cloned.1.call-start = ((), (), s32[]{:S(2)}) async-start(), calls=%async_computation.2 | async-start | bytes 4866048 | tf_op jit(solution)/shard_map/all_gather | solution.py:25
  7.9 156.0 %reduce-scatter.4.cloned.1.call-start = ((), (), s32[]{:S(2)}) async-start(), calls=%async_computation.5 | async-start | bytes 491520
  18.5 118.3 %copy-start.1 = (s32[1,192]{1,0:T(1,128)S(1)}, s32[1,192]{1,0:T(1,128)}, u32[]{:S(2)}) copy-start(s32[1,192]{1,0:T(1,128)} %param.5) | copy-start | bytes 2308
  126.8 10.8 %copy-start = (bf16[1,192,128]{2,1,0:T(8,128)(2,1)S(1)}, bf16[1,192,128]{2,1,0:T(8,128)(2,1)}, u32[]{:S(2)}) copy-start(bf16[1,192,128]{2,1,0:T(8,128)(2,1)} %param.7) | copy-start | bytes 147460
  139.7 196.7 %all-gather.6.cloned.1.call-start = ((), (), s32[]{:S(2)}) async-start(), calls=%async_computation.3 | async-start | bytes 4866048 | tf_op jit(solution)/shard_map/all_gather | solution.py:58
  165.7 298.3 %all-reduce.3.cloned.1.call-start = ((), (), s32[]{:S(2)}) async-start(), calls=%async_computation.4 | async-start | bytes 294912 | tf_op jit(solution)/shard_map/psum | solution.py:60
Sparse Core Ops, SparseCore 0:
  11.2 111.1 all-gather.3
  139.9 23.9 reduce-scatter.3
  168.1 168.2 all-gather.5
  341.7 122.2 all-reduce.2
where the time goes:
time: 473 us; the launch traced here: 472 us
  waiting for transfers between devices  302 us (64%)
  blocking collectives  122 us (26%)
  matrix products  16.9 us (4%)
  between operations  14.5 us (3%)
  local copies, waits for them, and re-layouts  14 us (3%)
    psum x1, waiting for transfers between devices, shards(): lax.psum(partial_grad.astype(jnp.bfloat16), ('dp', 'seq'))  117 us
    all_to_all x1, blocking collectives, shards(): lax.all_to_all(features, 'fsdp', split_axis=1, concat_axis=0, tiled=True)  105 us
    all_gather x1, waiting for transfers between devices, shards(): full_weight = lax.all_gather(qkv_weight, 'fsdp', axis=0, tiled=True)  104 us
    all_gather x1, waiting for transfers between devices, shards(): lax.all_gather(grad_heads, 'fsdp', axis=0, tiled=True)  57 us
    unnamed x5, waiting for transfers between devices  24.5 us
    all_gather x1, blocking collectives, shards(): lax.all_gather(own_pairs, 'seq', axis=0, tiled=True)  9.94 us
  transfers between devices with their start and end apart: 4, of which 4 were waited for; matrix products, arithmetic and copies ran while one was open for 3% of the time, Pallas kernels for 0%

commit v1 on v0

--- a/solution.py
+++ b/solution.py
@@ -57,7 +57,9 @@
     columns = lax.all_to_all(features, "fsdp", split_axis=1, concat_axis=0, tiled=True)
     partial_grad = contract_first(columns, lax.all_gather(grad_heads, "fsdp", axis=0, tiled=True))
     input_grad = contract_last(grad_heads, full_weight).astype(jnp.bfloat16)
-    weight_grad = lax.psum(partial_grad.astype(jnp.bfloat16), ("dp", "seq")).astype(jnp.float32)
+    weight_grad = lax.psum(lax.psum(partial_grad.astype(jnp.bfloat16), "seq"), "dp").astype(
+        jnp.float32
+    )
     return (input_grad[None], weight_grad)
 
 

time: 473 us -> 449 us (0.949)
  waiting for transfers between devices: 302 us -> 279 us
    psum x1 -> x2, waiting for transfers between devices: 117 us -> 93.3 us  [the longest x1 47.6 us: shards(): lax.psum(partial_grad.astype(jnp.bfloat16), 'seq')]
    unnamed x5 -> x6, waiting for transfers between devices: 24.5 us -> 24.5 us
  transfers between devices with their start and end apart: 4 -> 5, of which waited for: 4 -> 5; matrix products, arithmetic and copies ran while one was open for 3% -> 3% of each run, Pallas kernels for 0% -> 0%
where the time goes in v1:
time: 449 us
  waiting for transfers between devices  279 us (62%)
  blocking collectives  122 us (27%)
  matrix products  16.9 us (4%)
  between operations  14.6 us (3%)
  local copies, waits for them, and re-layouts  14 us (3%)
    all_to_all x1, blocking collectives, shards(): lax.all_to_all(features, 'fsdp', split_axis=1, concat_axis=0, tiled=True)  105 us
    all_gather x1, waiting for transfers between devices, shards(): full_weight = lax.all_gather(qkv_weight, 'fsdp', axis=0, tiled=True)  104 us
    all_gather x1, waiting for transfers between devices, shards(): lax.all_gather(grad_heads, 'fsdp', axis=0, tiled=True)  57 us
    psum x1, waiting for transfers between devices, shards(): lax.psum(partial_grad.astype(jnp.bfloat16), 'seq')  47.6 us
    psum x1, waiting for transfers between devices, shards(): lax.psum(lax.psum(partial_grad.astype(jnp.bfloat16), 'seq'), 'dp')  45.7 us
    unnamed x6, waiting for transfers between devices  24.5 us
    all_gather x1, blocking collectives, shards(): lax.all_gather(own_pairs, 'seq', axis=0, tiled=True)  9.94 us
  transfers between devices with their start and end apart: 5, of which 5 were waited for; matrix products, arithmetic and copies ran while one was open for 3% of the time, Pallas kernels for 0%

profile of v1, /device:TPU:1, one launch (start us, length us, event | category | flops | bytes accessed | tf_op | source)
XLA Modules:
  0.0 448.7 jit_solution(16543935629076641330)
XLA Ops:
  7.2 0.7 all-gather.4.cloned.1.call-update
  7.9 1.3 dynamic-slice
  9.9 0.9 dynamic-update-slice
  10.8 7.7 %all-reduce = s32[768]{0:T(1024)S(1)} all-reduce(s32[768]{0:T(1024)S(1)} %dynamic-update-slice), channel_id=2, replica_groups=mesh['dp'=4,'seq'=4,'fsdp'=32] {'seq'}, use_global_device_ids=true, to_apply=%add | all-reduce | flops 768 | bytes 6144
  18.5 103.9 %all-gather.4.cloned.1.call-done = bf16[6144,384]{1,0:T(8,128)(2,1)} async-done(((bf16[192,384]{1,0:T(8,128)(2,1)}), bf16[6144,384]{1,0:T(8,128)(2,1)}) %all-gather.4.cloned.1.call-update) | async-done | bytes 4718608 | tf_op jit(solution)/shard_map/all_gather | solution.py:25
  122.4 4.4 fusion.7
  126.8 9.9 %all_gather.14 = bf16[768,256]{1,0:T(8,128)(2,1)S(1)} all-gather(bf16[192,256]{1,0:T(8,128)(2,1)S(1)} %slice.17), channel_id=1, replica_groups=mesh['dp'=4,'seq'=4,'fsdp'=32] {'seq'}, dimensions={0}, use_global_device_ids=true | all-gather | bytes 491520 | tf_op jit(solution)/shard_map/all_gather | solution.py:31
  136.8 0.3 fusion.12
  137.9 0.3 fusion.11
  138.2 0.3 fusion.6
  138.8 0.9 copy.13
  140.1 23.7 %reduce-scatter.4.cloned.1.call-done = bf16[192,256]{1,0:T(8,128)(2,1)} async-done(((bf16[768,256]{1,0:T(8,128)(2,1)}), bf16[192,256]{1,0:T(8,128)(2,1)}) %reduce-scatter.4.cloned.1.call-update) | async-done | bytes 98320
  163.9 1.0 copy.14
  164.9 0.8 copy.10
  165.8 3.0 copy.11
  168.8 104.6 %all_to_all.19 = bf16[192,32,192]{0,2,1:T(8,128)(2,1)S(1)} all-to-all(bf16[192,32,192]{0,2,1:T(8,128)(2,1)S(1)} %bitcast.39), channel_id=1, replica_groups=mesh['dp'=4,'seq'=4,'fsdp'=32] {'fsdp'}, dimensions={1} | all-to-all | bytes 4718592 | tf_op jit(solution)/shard_map/all_to_all | solution.py:57
  273.4 1.8 copy.12
  275.2 4.2 all_to_all.17
  279.4 57.0 %all-gather.6.cloned.1.call-done = bf16[6144,384]{1,0:T(8,128)(2,1)} async-done(((bf16[192,384]{1,0:T(8,128)(2,1)}), bf16[6144,384]{1,0:T(8,128)(2,1)}) %all-gather.6.cloned.1.call-update) | async-done | bytes 4718608 | tf_op jit(solution)/shard_map/all_gather | solution.py:58
  336.4 5.1 %fusion.10 = bf16[192,384]{1,0:T(8,128)(2,1)} fusion(bf16[6144,192]{0,1:T(8,128)(2,1)} %all_to_all.17, bf16[6144,384]{1,0:T(8,128)(2,1)} %all-gather.6.cloned.1.call-done), kind=kOutput, calls=%fused_computation.14 | convolution fusion | flops 906043392 | bytes 7225344 | tf_op jit(solution)/shard_map/dot_general | solution.py:8
  341.6 47.6 %all-reduce.4.cloned.1.call-done = bf16[192,384]{1,0:T(8,128)(2,1)} async-done(((bf16[192,384]{1,0:T(8,128)(2,1)}), bf16[192,384]{1,0:T(8,128)(2,1)}) %all-reduce.4.cloned.1.call-update) | async-done | bytes 147472 | tf_op jit(solution)/shard_map/psum | solution.py:60
  389.2 5.6 %fusion = bf16[1,192,6144]{2,1,0:T(8,128)(2,1)} fusion(bf16[6144,384]{1,0:T(8,128)(2,1)} %all-gather.4.cloned.1.call-done, bf16[192,256]{0,1:T(8,128)(2,1)S(1)} %copy.14, bf16[192,128]{0,1:T(8,128)(2,1)S(1)} %copy.9), kind=kOutput, calls=%fused_computation.1 | convolution fusion | flops 907444224 | bytes 7225344 | tf_op jit(solution)/shard_map/dot_general | solution.py:14
  394.8 45.7 %all-reduce.6.cloned.1.call-done = bf16[192,384]{1,0:T(8,128)(2,1)} async-done(((bf16[192,384]{1,0:T(8,128)(2,1)}), bf16[192,384]{1,0:T(8,128)(2,1)}) %all-reduce.6.cloned.1.call-update) | async-done | bytes 147472 | tf_op jit(solution)/shard_map/psum | solution.py:60
  440.5 1.6 convert_element_type.36
  (24 shorter events, 1.7 us)
Async XLA Ops:
  7.2 115.2 %all-gather.4.cloned.1.call-start = ((), (), s32[]{:S(2)}) async-start(), calls=%async_computation.2 | async-start | bytes 4866048 | tf_op jit(solution)/shard_map/all_gather | solution.py:25
  7.9 156.0 %reduce-scatter.4.cloned.1.call-start = ((), (), s32[]{:S(2)}) async-start(), calls=%async_computation.6 | async-start | bytes 491520
  18.5 118.3 %copy-start.1 = (s32[1,192]{1,0:T(1,128)S(1)}, s32[1,192]{1,0:T(1,128)}, u32[]{:S(2)}) copy-start(s32[1,192]{1,0:T(1,128)} %param.5) | copy-start | bytes 2308
  126.8 10.8 %copy-start = (bf16[1,192,128]{2,1,0:T(8,128)(2,1)S(1)}, bf16[1,192,128]{2,1,0:T(8,128)(2,1)}, u32[]{:S(2)}) copy-start(bf16[1,192,128]{2,1,0:T(8,128)(2,1)} %param.7) | copy-start | bytes 147460
  139.7 196.7 %all-gather.6.cloned.1.call-start = ((), (), s32[]{:S(2)}) async-start(), calls=%async_computation.3 | async-start | bytes 4866048 | tf_op jit(solution)/shard_map/all_gather | solution.py:58
  165.7 223.5 %all-reduce.4.cloned.1.call-start = ((), (), s32[]{:S(2)}) async-start(), calls=%async_computation.4 | async-start | bytes 294912 | tf_op jit(solution)/shard_map/psum | solution.py:60
  341.5 99.0 %all-reduce.6.cloned.1.call-start = ((), (), s32[]{:S(2)}) async-start(), calls=%async_computation.5 | async-start | bytes 294912 | tf_op jit(solution)/shard_map/psum | solution.py:60
Sparse Core Ops, SparseCore 0:
  11.2 111.1 all-gather.3
  139.9 23.9 reduce-scatter.3
  168.1 168.2 all-gather.5
  341.6 47.4 all-reduce.3
  392.0 48.5 all-reduce.5
